TPU v7x, 256 devices: a whole 4x4x8 slice. The times are simulated.
256 devices in a mesh: req: 64 (over z, x, core), kv: 4 (over y).
Axes of the slice: x: 4, y: 4, z: 8, core: 2. Of those that a mesh axis runs over, the one named last changes fastest.
Arguments:
- residual_in: bfloat16 [128, 2560], P('req', 'kv'), may hold values from -8 to 8
- queries: bfloat16 [128, 2560], P('req', 'kv'), may hold values from -480 to 480
- fresh_token_keys: bfloat16 [128, 512], P('req', 'kv'), may hold values from -6 to 6
- fresh_token_values: bfloat16 [128, 512], P('req', 'kv'), may hold values from -6 to 6
- cached_key_slots: bfloat16 [128, 4096, 512], P('req', None, 'kv'), may hold values from -6 to 6
- cached_value_slots: bfloat16 [128, 4096, 512], P('req', None, 'kv'), may hold values from -6 to 6
- lengths: int32 [128], replicated, may hold values from 1 to 4096, as said below
- slot_order: int32 [128], replicated, may hold values from 0 to 127, as said below
- out_proj: bfloat16 [2560, 2560], P('kv'), may hold values from -0.5 to 0.5
- norm_gain: bfloat16 [2560], P('kv'), may hold values from 0.5 to 1.5
- expert_ids: int32 [128, 6], replicated, may hold values from 0 to 63, all different within a row; in each aligned block of 128 rows (0 to 127, 128 to 255, ...) at most 24 rows name the same one
- gate_values: float32 [128, 6], replicated, may hold values from 0.1 to 0.5
- gate_proj: bfloat16 [64, 2560, 1536], P('req', None, 'kv'), may hold values from -0.125 to 0.125
- up_proj: bfloat16 [64, 2560, 1536], P('req', None, 'kv'), may hold values from -0.125 to 0.125
- down_proj: bfloat16 [64, 1536, 2560], P('req', 'kv'), may hold values from -0.15625 to 0.15625
Outputs:
- layer_out: bfloat16 [128, 2560], P('req', 'kv')
Inputs may be any that keep to these rules, and one draw needn't show every extreme that they name: `lengths`: each request's count of cached positions; some request has exactly 4096. A permutation of the requests: slot s serves request slot_order[s], and cached_key_slots[s], cached_value_slots[s] hold that request's cache. Requests sorted by decreasing length are dealt to the 64 groups of 2 consecutive slots, one round forward, the next backward. `expert_ids`: each token names 6 different experts; no expert is named by more than 24 tokens, a bound that some block reaches.
All inputs are finite; a program needn't handle non-finite values.
Results may differ from a plain program's by a relative error of at most 0.012.
Values may be sent and summed in bfloat16 or wider, within the bound.
No kernel may reach another device: no remote copies, remote signals or barrier semaphores. Data moves between devices by JAX's collectives and lax.ppermute only.
A program may use at most 64 MiB of HBM per device.

v0:
```python
import math
import jax
import jax.numpy as jnp
from jax import lax
from jax.sharding import PartitionSpec as P


def device_blocks(term, groups, parts):
    row_count = term.shape[0] // groups
    col_count = term.shape[1] // parts
    return (
        term.reshape(groups, row_count, parts, col_count)
        .transpose(0, 2, 1, 3)
        .reshape(groups * parts * row_count, col_count)
    )


def per_device(
    residual_in,
    queries,
    fresh_token_keys,
    fresh_token_values,
    cached_key_slots,
    cached_value_slots,
    lengths,
    slot_order,
    out_proj,
    norm_gain,
    expert_ids,
    gate_values,
    gate_proj,
    up_proj,
    down_proj,
):
    req_count = lax.axis_size("req")
    kv_count = lax.axis_size("kv")
    req_index = lax.axis_index("req")
    per_dev = residual_in.shape[0]
    head_dim = fresh_token_keys.shape[1]
    total_reqs = lengths.shape[0]
    model_width = out_proj.shape[1]
    all_queries, all_keys, all_values = (
        lax.all_gather(queries, "req", axis=0, tiled=True),
        lax.all_gather(fresh_token_keys, "req", axis=0, tiled=True),
        lax.all_gather(fresh_token_values, "req", axis=0, tiled=True),
    )
    served = lax.dynamic_slice_in_dim(slot_order, req_index * per_dev, per_dev)
    query_rows = all_queries[served].reshape(per_dev, -1, head_dim)
    self_key_row = all_keys[served]
    self_value_row = all_values[served]
    live_len = lengths[served]
    inv_root = 1.0 / math.sqrt(head_dim)
    scores = (
        jnp.einsum("rqd,rld->rql", query_rows, cached_key_slots, preferred_element_type=jnp.float32)
        * inv_root
    )
    positions = jnp.arange(cached_key_slots.shape[1])
    scores = jnp.where((positions[None, :] < live_len[:, None])[:, None, :], scores, -1e30)
    own_score = (
        jnp.einsum("rqd,rd->rq", query_rows, self_key_row, preferred_element_type=jnp.float32)
        * inv_root
    )
    highest = jnp.maximum(jnp.max(scores, axis=2), own_score)
    weights = jnp.exp(scores - highest[:, :, None])
    own_weight = jnp.exp(own_score - highest)
    totals = jnp.sum(weights, axis=2) + own_weight
    numerator = jnp.einsum(
        "rql,rld->rqd",
        weights.astype(jnp.bfloat16),
        cached_value_slots,
        preferred_element_type=jnp.float32,
    )
    own_low = lax.optimization_barrier(own_weight.astype(jnp.bfloat16)).astype(jnp.float32)
    numerator = numerator + own_low[:, :, None] * self_value_row.astype(jnp.float32)[:, None, :]
    attended = (numerator / totals[:, :, None]).astype(jnp.bfloat16).reshape(per_dev, -1)
    projected = jnp.dot(attended, out_proj, preferred_element_type=jnp.float32)
    placed = jnp.zeros((total_reqs, model_width), jnp.float32).at[served].set(projected)
    attn_part = lax.psum_scatter(
        device_blocks(placed, req_count, kv_count), ("req", "kv"), scatter_dimension=0, tiled=True
    )
    hidden = residual_in.astype(jnp.float32) + attn_part
    squares = lax.psum(jnp.sum(hidden * hidden, axis=1), "kv")
    normed = (
        hidden * lax.rsqrt(squares / model_width + 1e-06)[:, None] * norm_gain.astype(jnp.float32)
    ).astype(jnp.bfloat16)
    gathered = lax.all_gather(normed, ("req", "kv"), axis=0, tiled=True)
    tokens = (
        gathered.reshape(req_count, kv_count, per_dev, -1)
        .transpose(0, 2, 1, 3)
        .reshape(total_reqs, -1)
    )
    local_count = gate_proj.shape[0]
    capacity = min(2 * total_reqs * expert_ids.shape[1] // (local_count * req_count), total_reqs)
    expert = req_index * local_count + 0
    named_here = expert_ids == expert
    token_gate = jnp.sum(jnp.where(named_here, gate_values, 0.0), axis=1)
    uses_expert = jnp.any(named_here, axis=1)
    picked = jnp.nonzero(uses_expert, size=capacity, fill_value=0)[0].astype(jnp.int32)
    valid_rows = jnp.arange(capacity) < jnp.sum(uses_expert.astype(jnp.int32))
    row_block = tokens[picked]
    gate_h = jnp.dot(row_block, gate_proj[0], preferred_element_type=jnp.float32)
    up_h = jnp.dot(row_block, up_proj[0], preferred_element_type=jnp.float32)
    inner_act = (jax.nn.silu(gate_h) * up_h).astype(jnp.bfloat16)
    outputs = jnp.dot(inner_act, down_proj[0], preferred_element_type=jnp.float32)
    row_gate = jnp.where(valid_rows, token_gate[picked], 0.0)
    weighted_list = [outputs * row_gate[:, None]]
    picked_list = [picked]
    stacked_rows = jnp.concatenate(weighted_list, axis=0)
    stacked_idx = jnp.concatenate(picked_list, axis=0)
    mixture = jnp.zeros((total_reqs, model_width), jnp.float32).at[stacked_idx].add(stacked_rows)
    moe_part = lax.psum_scatter(
        device_blocks(mixture, req_count, kv_count), ("req", "kv"), scatter_dimension=0, tiled=True
    )
    return (hidden + moe_part).astype(jnp.bfloat16)


def solution(mesh):
    in_specs = (
        P("req", "kv"),
        P("req", "kv"),
        P("req", "kv"),
        P("req", "kv"),
        P("req", None, "kv"),
        P("req", None, "kv"),
        P(),
        P(),
        P("kv", None),
        P("kv"),
        P(),
        P(),
        P("req", None, "kv"),
        P("req", None, "kv"),
        P("req", "kv", None),
    )
    out_specs = P("req", "kv")
    return jax.shard_map(
        per_device, mesh=mesh, in_specs=in_specs, out_specs=out_specs, check_vma=False
    )
```

profile of v0, /device:TPU:2, one launch (start us, length us, event | category | flops | bytes accessed | tf_op | source)
XLA Modules:
  0.0 775.9 jit_solution(7634944071850056132)
XLA Ops:
  7.4 1.4 gather_fusion
  8.9 42.3 %all-gather.1 = bf16[64,2,128]{2,1,0:T(2,128)(2,1)S(1)} all-gather(bf16[1,2,128]{2,1,0:T(2,128)(2,1)} %bitcast.58), channel_id=1, replica_groups=mesh['req'=64,'kv'=4] {'req'}, dimensions={0}, use_global_device_ids=true | all-gather | bytes 33280 | tf_op jit(solution)/shard_map/all_gather | solution.py:44
  51.8 37.5 %all-gather.2 = bf16[64,2,128]{2,1,0:T(2,128)(2,1)S(1)} all-gather(bf16[1,2,128]{2,1,0:T(2,128)(2,1)} %bitcast.59), channel_id=1, replica_groups=mesh['req'=64,'kv'=4] {'req'}, dimensions={0}, use_global_device_ids=true | all-gather | bytes 33280 | tf_op jit(solution)/shard_map/all_gather | solution.py:45
  89.9 41.7 %all-gather = bf16[64,2,640]{2,1,0:T(2,128)(2,1)S(1)} all-gather(bf16[1,2,640]{2,1,0:T(2,128)(2,1)} %bitcast.57), channel_id=1, replica_groups=mesh['req'=64,'kv'=4] {'req'}, dimensions={0}, use_global_device_ids=true | all-gather | bytes 166400 | tf_op jit(solution)/shard_map/all_gather | solution.py:43
  132.3 1.5 gather_fusion.1
  134.0 2.4 fusion.47
  137.6 1.8 scatter_custom_fusion
  139.4 2.7 reshape.153
  142.1 3.1 copy.27
  145.2 3.1 reshape.154
  148.8 1.4 scatter_custom_fusion.1
  153.2 255.0 %all-reduce.5.cloned.1.call-done = f32[512,640]{1,0:T(8,128)} async-done(((f32[512,640]{1,0:T(8,128)}), f32[512,640]{1,0:T(8,128)}) %all-reduce.5.cloned.1.call-update) | async-done | bytes 1310736
  409.0 10.2 %psum.7 = f32[2]{0:T(128)S(1)} all-reduce(f32[2]{0:T(128)S(1)} %multiply_reduce_fusion), channel_id=1, replica_groups=mesh['req'=64,'kv'=4] {'kv'}, use_global_device_ids=true, to_apply=%region_10.11 | all-reduce | flops 2 | bytes 16 | tf_op jit(solution)/shard_map/psum | solution.py:82
  420.0 70.2 %all-gather.3 = bf16[256,2,640]{2,1,0:T(2,128)(2,1)S(1)} all-gather(bf16[1,2,640]{2,1,0:T(2,128)(2,1)S(1)} %fusion.39), channel_id=1, replica_groups=mesh['req'=64,'kv'=4] {'req','kv'}, dimensions={0}, use_global_device_ids=true | all-gather | bytes 657920 | tf_op jit(solution)/shard_map/all_gather | solution.py:86
  490.5 0.9 copy.35
  491.4 1.9 gather_fusion.4
  493.3 1.9 fusion.4
  495.2 3.8 convolution_multiply_fusion.1
  499.0 2.5 scatter_custom_fusion.2
  501.5 2.7 reshape.158
  504.2 3.1 copy.31
  507.3 3.1 reshape.159
  510.3 257.4 %all-reduce.7.cloned.1.call-done = f32[512,640]{1,0:T(8,128)} async-done(((f32[512,640]{1,0:T(8,128)}), f32[512,640]{1,0:T(8,128)}) %all-reduce.7.cloned.1.call-update) | async-done | bytes 1310736
  767.7 1.3 fusion.35
  (50 shorter events, 9.5 us)
Async XLA Ops:
  6.5 130.6 %copy-start = (bf16[640,2560]{1,0:T(8,128)(2,1)S(1)}, bf16[640,2560]{1,0:T(8,128)(2,1)}, u32[]{:S(2)}) copy-start(bf16[640,2560]{1,0:T(8,128)(2,1)} %param.23) | copy-start | bytes 9830404
  6.5 401.6 %all-reduce.5.cloned.1.call-start = ((), (), s32[]{:S(2)}) async-start(), calls=%async_computation | async-start | bytes 2621440
  133.8 2.8 copy-start.1
  145.2 3.2 copy-start.3
  145.2 3.2 copy-start.4
  145.2 263.0 %copy-start.2 = (bf16[2,640]{1,0:T(2,128)(2,1)S(1)}, bf16[2,640]{1,0:T(2,128)(2,1)}, u32[]{:S(2)}) copy-start(bf16[2,640]{1,0:T(2,128)(2,1)} %param.15) | copy-start | bytes 7684
  145.2 263.8 %copy-start.5 = (bf16[640]{0:T(1024)(128)(2,1)S(1)}, bf16[640]{0:T(1024)(128)(2,1)}, u32[]{:S(2)}) copy-start(bf16[640]{0:T(1024)(128)(2,1)} %param.24) | copy-start | bytes 3844
  148.3 619.4 %all-reduce.7.cloned.1.call-start = ((), (), s32[]{:S(2)}) async-start(), calls=%async_computation.1 | async-start | bytes 2621440
Sparse Core Ops, SparseCore 0:
  148.4 259.6 all-reduce.4
  510.5 257.1 all-reduce.6
where the time goes:
time: 777 us; the launch traced here: 776 us
  waiting for transfers between devices  512 us (66%)
  blocking collectives  202 us (26%)
  local copies, waits for them, and re-layouts  28.2 us (4%)
  between operations  13.5 us (2%)
  other arithmetic  10.5 us (1%)
  matrix products  9.24 us (1%)
    unnamed x4, waiting for transfers between devices  512 us
    all_gather x1, blocking collectives, per_device(): gathered = lax.all_gather(normed, ('req', 'kv'), axis=0, tiled=True)  70.2 us
    all_gather x1, blocking collectives, per_device(): lax.all_gather(fresh_token_keys, 'req', axis=0, tiled=True)  42.3 us
    all_gather x1, blocking collectives, per_device(): lax.all_gather(queries, 'req', axis=0, tiled=True)  41.7 us
    all_gather x1, blocking collectives, per_device(): lax.all_gather(fresh_token_values, 'req', axis=0, tiled=True)  37.5 us
  transfers between devices with their start and end apart: 2, of which 2 were waited for; matrix products, arithmetic and copies ran while one was open for 1% of the time, Pallas kernels for 0%

commit v1 on v0

--- a/solution.py
+++ b/solution.py
@@ -40,7 +40,9 @@
     total_reqs = lengths.shape[0]
     model_width = out_proj.shape[1]
     all_queries, all_keys, all_values = (
-        lax.all_gather(queries, "req", axis=0, tiled=True),
+        jnp.concatenate(
+            lax.all_to_all(jnp.stack([queries] * lax.axis_size("req")), "req", 0, 0), axis=0
+        ),
         lax.all_gather(fresh_token_keys, "req", axis=0, tiled=True),
         lax.all_gather(fresh_token_values, "req", axis=0, tiled=True),
     )

time: 777 us -> 748 us (0.963)
  blocking collectives: 202 us -> 159 us
  starting transfers between devices: 0.04 us -> 12.1 us
    all_gather x1 -> x0, blocking collectives: 41.7 us -> none  [per_device(): lax.all_gather(queries, 'req', axis=0, tiled=True)]
    all_to_all x0 -> x1, starting transfers between devices: none -> 12 us  [per_device(): lax.all_to_all(jnp.stack([queries] * lax.axis_size('req')), 'req', 0, 0)]
  transfers between devices with their start and end apart: 2 -> 3, of which waited for: 2 -> 2; matrix products, arithmetic and copies ran while one was open for 1% -> 1% of each run, Pallas kernels for 0% -> 0%
where the time goes in v1:
time: 748 us; the launch traced here: 747 us
  waiting for transfers between devices  512 us (68%)
  blocking collectives  159 us (21%)
  local copies, waits for them, and re-layouts  30.3 us (4%)
  between operations  13.5 us (2%)
  starting transfers between devices  12.1 us (2%)
  other arithmetic  11.9 us (2%)
  matrix products  9.24 us (1%)
    unnamed x4, waiting for transfers between devices  512 us
    all_gather x1, blocking collectives, per_device(): gathered = lax.all_gather(normed, ('req', 'kv'), axis=0, tiled=True)  70.2 us
    all_gather x1, blocking collectives, per_device(): lax.all_gather(fresh_token_keys, 'req', axis=0, tiled=True)  40.6 us
    all_gather x1, blocking collectives, per_device(): lax.all_gather(fresh_token_values, 'req', axis=0, tiled=True)  37.5 us
  transfers between devices with their start and end apart: 3, of which 2 were waited for; matrix products, arithmetic and copies ran while one was open for 1% of the time, Pallas kernels for 0%

profile of v1, /device:TPU:2, one launch (start us, length us, event | category | flops | bytes accessed | tf_op | source)
XLA Modules:
  0.0 747.5 jit_solution(17851977969031239512)
XLA Ops:
  6.5 1.6 stack.2
  8.1 12.0 %all-to-all-start = ((bf16[64,2,640]{2,1,0:T(2,128)(2,1)}), bf16[64,2,640]{2,1,0:T(2,128)(2,1)S(1)}, u32[]{:S(2)}, u32[]{:S(2)}) async-start(bf16[64,2,640]{2,1,0:T(2,128)(2,1)} %stack.2), calls=%async_computation | async-start | bytes 327680 | tf_op jit(solution)/shard_map/all_to_all | solution.py:44
  20.9 1.3 gather_fusion
  23.0 40.6 %all-gather = bf16[64,2,128]{2,1,0:T(2,128)(2,1)S(1)} all-gather(bf16[1,2,128]{2,1,0:T(2,128)(2,1)} %bitcast.56), channel_id=1, replica_groups=mesh['req'=64,'kv'=4] {'req'}, dimensions={0}, use_global_device_ids=true | all-gather | bytes 33280 | tf_op jit(solution)/shard_map/all_gather | solution.py:46
  64.2 37.5 %all-gather.1 = bf16[64,2,128]{2,1,0:T(2,128)(2,1)S(1)} all-gather(bf16[1,2,128]{2,1,0:T(2,128)(2,1)} %bitcast.57), channel_id=1, replica_groups=mesh['req'=64,'kv'=4] {'req'}, dimensions={0}, use_global_device_ids=true | all-gather | bytes 33280 | tf_op jit(solution)/shard_map/all_gather | solution.py:47
  104.8 1.5 gather_fusion.1
  106.4 2.4 fusion.47
  110.1 1.8 scatter_custom_fusion
  111.9 2.7 reshape.159
  114.6 3.1 copy.27
  117.6 3.1 reshape.160
  120.9 1.4 scatter_custom_fusion.1
  125.2 254.5 %all-reduce.5.cloned.1.call-done = f32[512,640]{1,0:T(8,128)} async-done(((f32[512,640]{1,0:T(8,128)}), f32[512,640]{1,0:T(8,128)}) %all-reduce.5.cloned.1.call-update) | async-done | bytes 1310736
  380.6 10.2 %psum.7 = f32[2]{0:T(128)S(1)} all-reduce(f32[2]{0:T(128)S(1)} %multiply_reduce_fusion), channel_id=1, replica_groups=mesh['req'=64,'kv'=4] {'kv'}, use_global_device_ids=true, to_apply=%region_10.11 | all-reduce | flops 2 | bytes 16 | tf_op jit(solution)/shard_map/psum | solution.py:84
  391.6 70.2 %all-gather.2 = bf16[256,2,640]{2,1,0:T(2,128)(2,1)S(1)} all-gather(bf16[1,2,640]{2,1,0:T(2,128)(2,1)S(1)} %fusion.39), channel_id=1, replica_groups=mesh['req'=64,'kv'=4] {'req','kv'}, dimensions={0}, use_global_device_ids=true | all-gather | bytes 657920 | tf_op jit(solution)/shard_map/all_gather | solution.py:88
  463.0 1.9 gather_fusion.4
  464.9 1.9 fusion.4
  466.8 3.8 convolution_multiply_fusion.1
  470.6 2.5 scatter_custom_fusion.2
  473.1 2.7 reshape.164
  475.8 3.1 copy.31
  478.9 3.1 reshape.165
  481.9 257.4 %all-reduce.7.cloned.1.call-done = f32[512,640]{1,0:T(8,128)} async-done(((f32[512,640]{1,0:T(8,128)}), f32[512,640]{1,0:T(8,128)}) %all-reduce.7.cloned.1.call-update) | async-done | bytes 1310736
  739.3 1.3 fusion.35
  (48 shorter events, 12.5 us)
Async XLA Ops:
  6.5 103.0 %copy-start = (bf16[640,2560]{1,0:T(8,128)(2,1)S(1)}, bf16[640,2560]{1,0:T(8,128)(2,1)}, u32[]{:S(2)}) copy-start(bf16[640,2560]{1,0:T(8,128)(2,1)} %param.23) | copy-start | bytes 9830404
  8.1 96.0 %all-to-all-start = ((bf16[64,2,640]{2,1,0:T(2,128)(2,1)}), bf16[64,2,640]{2,1,0:T(2,128)(2,1)S(1)}, u32[]{:S(2)}, u32[]{:S(2)}) async-start(bf16[64,2,640]{2,1,0:T(2,128)(2,1)} %stack.2), calls=%async_computation | async-start | bytes 327680 | tf_op jit(solution)/shard_map/all_to_all | solution.py:44
  20.1 359.6 %all-reduce.5.cloned.1.call-start = ((), (), s32[]{:S(2)}) async-start(), calls=%async_computation.1 | async-start | bytes 2621440
  106.3 2.8 copy-start.1
  117.6 262.1 %copy-start.2 = (bf16[2,640]{1,0:T(2,128)(2,1)S(1)}, bf16[2,640]{1,0:T(2,128)(2,1)}, u32[]{:S(2)}) copy-start(bf16[2,640]{1,0:T(2,128)(2,1)} %param.15) | copy-start | bytes 7684
  117.6 262.9 %copy-start.3 = (bf16[640]{0:T(1024)(128)(2,1)S(1)}, bf16[640]{0:T(1024)(128)(2,1)}, u32[]{:S(2)}) copy-start(bf16[640]{0:T(1024)(128)(2,1)} %param.24) | copy-start | bytes 3844
  120.7 618.6 %all-reduce.7.cloned.1.call-start = ((), (), s32[]{:S(2)}) async-start(), calls=%async_computation.2 | async-start | bytes 2621440
Sparse Core Ops, SparseCore 0:
  120.9 258.8 all-reduce.4
  482.1 257.1 all-reduce.6
